TPU v7x, 128 devices: a whole 4x4x4 slice. The times are simulated.
128 devices in a mesh: col: 8 (over y, z_hi), pair: 16 (over x, z_lo, core).
Axes of the slice: x: 4, y: 4, z: 4 (z_hi: 2, z_lo: 2; z = z_hi * 2 + z_lo), core: 2. Of those that a mesh axis runs over, the one named last changes fastest.
Arguments:
- integrals: bfloat16 [512, 128, 128], P('pair', 'col'), may hold values from -6 to 6
- pno_energy: float32 [512, 128], P('pair'), may hold values from 0.5 to 4
- shift: float32 [512], P('pair'), may hold values from 0.5 to 2
- intersections: bfloat16 [512, 128, 128, 128], P('pair', 'col'), may hold values from -0.09375 to 0.09375
- links: int32 [512, 128], P('pair', 'col'), may hold values from 0 to 63
- counts: int32 [512], P('pair'), may hold values from 1 to 128, as said below
- column_of: int32 [512], P('pair'), may hold values from 0 to 63
Outputs:
- amplitudes: float32 [512, 128, 128], P('pair', 'col')
- pair_energy: float32 [512], P('pair')
Inputs may be any that keep to these rules, and one draw needn't show every extreme that they name: Pair p couples through its first counts[p] slots; later slots are unused.
All inputs are finite; a program needn't handle non-finite values.
Results may differ from a plain program's by a relative error of at most 0.0012.
Values may be sent and summed in bfloat16 or wider, within the bound.
No kernel may reach another device: no remote copies, remote signals or barrier semaphores. Data moves between devices by JAX's collectives and lax.ppermute only.
A program may use at most 192 MiB of HBM per device.

v0:
```python
import jax
import jax.numpy as jnp
from jax import lax
from jax.sharding import PartitionSpec as P

COL_DEV = 8
SWEEPS = 3


def per_device(integrals, pno_energy, shift, intersections, links, counts, column_of):
    pair_dev = integrals.shape[0]
    row_count = integrals.shape[1]
    width = integrals.shape[2]
    slot_dev = intersections.shape[1]
    col_size = lax.axis_size("col")
    ncol_all = COL_DEV * col_size
    rank = lax.axis_index("col")
    row_energy = lax.dynamic_slice_in_dim(pno_energy, rank * row_count, row_count, 1)
    denom = row_energy[:, :, None] + pno_energy[:, None, :] + shift[:, None, None]
    kfloat = integrals.astype(jnp.float32)
    amplitudes = -kfloat / denom
    one_hot = (jnp.arange(ncol_all, dtype=jnp.int32)[:, None] == column_of[None, :]).astype(
        jnp.float32
    )
    own_tiles, own_links = (intersections, links)
    slot_ids = rank * slot_dev + jnp.arange(slot_dev, dtype=jnp.int32)
    own_live = (slot_ids[None, :] < counts[:, None]).astype(jnp.float32)
    for sweep in range(SWEEPS):
        contrib = jnp.dot(
            one_hot,
            amplitudes.reshape(pair_dev, row_count * width),
            precision=lax.Precision.HIGHEST,
        )
        contrib = contrib.reshape(ncol_all, row_count, width)
        totals = lax.psum(contrib, "pair")
        colamp = lax.all_gather(totals.astype(jnp.bfloat16), "col", axis=1, tiled=True)
        selected = colamp[own_links]
        left = jnp.einsum(
            "pmab,pmbc->pmac", own_tiles, selected, preferred_element_type=jnp.float32
        ).astype(jnp.bfloat16)
        right = jnp.einsum("pmac,pmdc->pmad", left, own_tiles, preferred_element_type=jnp.float32)
        partial_sum = jnp.sum(right * own_live[:, :, None, None], axis=1)
        coupled = lax.psum_scatter(partial_sum, "col", scatter_dimension=1, tiled=True)
        amplitudes = -(kfloat + coupled) / denom
    pair_energy = lax.psum(jnp.sum(kfloat * amplitudes, axis=(1, 2)), "col")
    return (amplitudes, pair_energy)


def solution(mesh):
    placed = (
        P("pair", "col", None),
        P("pair", None),
        P("pair"),
        P("pair", "col", None, None),
        P("pair", "col"),
        P("pair"),
        P("pair"),
    )
    return jax.shard_map(
        per_device,
        mesh=mesh,
        in_specs=placed,
        out_specs=(P("pair", "col", None), P("pair")),
        check_vma=False,
    )
```

profile of v0, /device:TPU:0, one launch (start us, length us, event | category | flops | bytes accessed | tf_op | source)
XLA Modules:
  0.0 745.7 jit_solution(13268401989379443307)
XLA Ops:
  7.2 0.0 all-gather.4.cloned.1.call-start
  7.2 0.8 constant_dynamic-slice_fusion
  8.0 1.1 fusion.18
  9.1 1.1 fusion.32
  10.3 62.5 %all-reduce.3 = bf16[64,16,128]{2,0,1:T(8,128)(2,1)} all-reduce(f32[64,16,128]{2,0,1:T(8,128)S(1)} %fusion.32), channel_id=1, replica_groups=mesh['col'=8,'pair'=16] {'pair'}, use_global_device_ids=true, to_apply=%region_0.0 | all-reduce | flops 131072 | bytes 786432 | tf_op jit(solution)/shard_map/psum | solution.py:35
  72.7 0.0 all-gather.4.cloned.1.call-update
  72.8 0.0 reduce-scatter.4.cloned.1.call-start
  72.8 0.7 compare_select_fusion
  73.5 0.1 copy.17
  73.6 0.1 reshape.61
  73.7 0.7 compare_convert_fusion
  74.4 52.9 %all-gather.4.cloned.1.call-done = bf16[64,128,128]{2,0,1:T(8,128)(2,1)} async-done(((bf16[64,16,128]{2,0,1:T(8,128)(2,1)}), bf16[64,128,128]{2,0,1:T(8,128)(2,1)}) %all-gather.4.cloned.1.call-update) | async-done | bytes 2097168 | tf_op jit(solution)/shard_map/all_gather | solution.py:36
  127.3 2.9 copy.18
  130.2 13.9 %gather_fusion = bf16[512,128,128]{2,1,0:T(8,128)(2,1)} fusion(bf16[64,128,128]{2,1,0:T(8,128)(2,1)S(1)} %copy.18, s32[1024]{0:T(1024)S(1)} %pad_clamp_fusion), kind=kCustom, calls=%fused_computation | custom fusion | bytes 33556480 | tf_op jit(solution)/shard_map/gather | solution.py:37
  144.1 0.0 copy-start
  144.1 0.0 copy-start.1
  144.1 0.0 copy-start.2
  144.1 0.0 copy-start.3
  144.1 29.2 %multiply_reduce_fusion.2 = f32[32,128,128]{2,1,0:T(8,128)} fusion(f32[32,16]{1,0:T(8,128)S(1)} %compare_convert_fusion, bf16[32,16,128,128]{3,2,1,0:T(8,128)(2,1)} %param.10, bf16[32,16,128,128]{3,2,1,0:T(8,128)(2,1)} %bitcast.57), kind=kOutput, calls=%fused_computation.5 | convolution fusion | flops 4319608832 | bytes 35653632 | tf_op jit(solution)/shard_map/pmac,pmdc->pmad/dot_general | solution.py:41
  173.4 0.0 reduce-scatter.4.cloned.1.call-update
  173.4 0.0 all-gather.6.cloned.1.call-start
  173.4 74.5 %reduce-scatter.4.cloned.1.call-done = f32[32,16,128]{2,1,0:T(8,128)} async-done(((f32[32,128,128]{2,1,0:T(8,128)}), f32[32,16,128]{2,1,0:T(8,128)}) %reduce-scatter.4.cloned.1.call-update) | async-done | bytes 262160 | tf_op jit(solution)/shard_map/reduce_scatter | solution.py:43
  247.9 0.0 copy-done
  247.9 0.0 copy-done.1
  247.9 0.0 copy-done.2
  247.9 1.1 fusion.20
  249.1 0.0 copy-done.3
  249.1 0.5 fusion.29
  249.6 59.6 %all-reduce.4 = bf16[64,16,128]{2,0,1:T(8,128)(2,1)} all-reduce(f32[64,16,128]{2,0,1:T(8,128)S(1)} %fusion.29), channel_id=1, replica_groups=mesh['col'=8,'pair'=16] {'pair'}, use_global_device_ids=true, to_apply=%region_3.0 | all-reduce | flops 131072 | bytes 786432 | tf_op jit(solution)/shard_map/psum | solution.py:35
  309.1 0.0 all-gather.6.cloned.1.call-update
  309.2 0.2 reduce-scatter.6.cloned.1.call-start
  309.4 51.7 %all-gather.6.cloned.1.call-done = bf16[64,128,128]{2,0,1:T(8,128)(2,1)} async-done(((bf16[64,16,128]{2,0,1:T(8,128)(2,1)}), bf16[64,128,128]{2,0,1:T(8,128)(2,1)}) %all-gather.6.cloned.1.call-update) | async-done | bytes 2097168 | tf_op jit(solution)/shard_map/all_gather | solution.py:36
  361.1 2.9 copy.22
  364.0 13.9 %gather_fusion.1 = bf16[512,128,128]{2,1,0:T(8,128)(2,1)} fusion(bf16[64,128,128]{2,1,0:T(8,128)(2,1)S(1)} %copy.22, s32[1024]{0:T(1024)S(1)} %pad_clamp_fusion), kind=kCustom, calls=%fused_computation.1 | custom fusion | bytes 33556480 | tf_op jit(solution)/shard_map/gather | solution.py:37
  377.9 29.2 %multiply_reduce_fusion.1 = f32[32,128,128]{2,1,0:T(8,128)} fusion(f32[32,16]{1,0:T(8,128)S(1)} %compare_convert_fusion, bf16[32,16,128,128]{3,2,1,0:T(8,128)(2,1)} %param.10, bf16[32,16,128,128]{3,2,1,0:T(8,128)(2,1)} %bitcast.58), kind=kOutput, calls=%fused_computation.4 | convolution fusion | flops 4319608832 | bytes 35653632 | tf_op jit(solution)/shard_map/pmac,pmdc->pmad/dot_general | solution.py:41
  407.1 0.0 reduce-scatter.6.cloned.1.call-update
  407.1 0.0 all-gather.8.cloned.1.call-start
  407.2 74.3 %reduce-scatter.6.cloned.1.call-done = f32[32,16,128]{2,1,0:T(8,128)} async-done(((f32[32,128,128]{2,1,0:T(8,128)}), f32[32,16,128]{2,1,0:T(8,128)}) %reduce-scatter.6.cloned.1.call-update) | async-done | bytes 262160 | tf_op jit(solution)/shard_map/reduce_scatter | solution.py:43
  481.5 1.1 fusion.22
  482.7 0.5 fusion.26
  483.2 59.7 %all-reduce.5 = bf16[64,16,128]{2,0,1:T(8,128)(2,1)} all-reduce(f32[64,16,128]{2,0,1:T(8,128)S(1)} %fusion.26), channel_id=1, replica_groups=mesh['col'=8,'pair'=16] {'pair'}, use_global_device_ids=true, to_apply=%region_6.0 | all-reduce | flops 131072 | bytes 786432 | tf_op jit(solution)/shard_map/psum | solution.py:35
  542.8 0.0 all-gather.8.cloned.1.call-update
  542.8 0.3 reduce-scatter.8.cloned.1.call-start
  543.1 51.6 %all-gather.8.cloned.1.call-done = bf16[64,128,128]{2,0,1:T(8,128)(2,1)} async-done(((bf16[64,16,128]{2,0,1:T(8,128)(2,1)}), bf16[64,128,128]{2,0,1:T(8,128)(2,1)}) %all-gather.8.cloned.1.call-update) | async-done | bytes 2097168 | tf_op jit(solution)/shard_map/all_gather | solution.py:36
  594.8 2.9 copy.26
  597.7 13.9 %gather_fusion.2 = bf16[512,128,128]{2,1,0:T(8,128)(2,1)} fusion(bf16[64,128,128]{2,1,0:T(8,128)(2,1)S(1)} %copy.26, s32[1024]{0:T(1024)S(1)} %pad_clamp_fusion), kind=kCustom, calls=%fused_computation.2 | custom fusion | bytes 33556480 | tf_op jit(solution)/shard_map/gather | solution.py:37
  611.6 29.2 %multiply_reduce_fusion = f32[32,128,128]{2,1,0:T(8,128)} fusion(f32[32,16]{1,0:T(8,128)S(1)} %compare_convert_fusion, bf16[32,16,128,128]{3,2,1,0:T(8,128)(2,1)} %param.10, bf16[32,16,128,128]{3,2,1,0:T(8,128)(2,1)} %bitcast.56), kind=kOutput, calls=%fused_computation.3 | convolution fusion | flops 4319608832 | bytes 35653632 | tf_op jit(solution)/shard_map/pmac,pmdc->pmad/dot_general | solution.py:41
  640.8 0.0 reduce-scatter.8.cloned.1.call-update
  640.8 74.3 %reduce-scatter.8.cloned.1.call-done = f32[32,16,128]{2,1,0:T(8,128)} async-done(((f32[32,128,128]{2,1,0:T(8,128)}), f32[32,16,128]{2,1,0:T(8,128)}) %reduce-scatter.8.cloned.1.call-update) | async-done | bytes 262160 | tf_op jit(solution)/shard_map/reduce_scatter | solution.py:43
  715.2 2.2 fusion.25
  717.3 21.5 %psum.31 = f32[32]{0:T(128)} all-reduce(f32[32]{0:T(128)S(1)} %get-tuple-element.2), channel_id=1, replica_groups=mesh['col'=8,'pair'=16] {'col'}, use_global_device_ids=true, to_apply=%region_10.0 | all-reduce | flops 32 | bytes 256 | tf_op jit(solution)/shard_map/psum | solution.py:45
  (2 shorter events, 0.0 us)
Async XLA Ops:
  7.2 120.1 %all-gather.4.cloned.1.call-start = ((), (), s32[]{:S(2)}) async-start(), calls=%async_computation.3 | async-start | bytes 2359296 | tf_op jit(solution)/shard_map/all_gather | solution.py:36
  72.8 175.2 %reduce-scatter.4.cloned.1.call-start = ((), (), s32[]{:S(2)}) async-start(), calls=%async_computation.4 | async-start | bytes 2359296 | tf_op jit(solution)/shard_map/reduce_scatter | solution.py:43
  144.1 103.8 %copy-start = (bf16[32,16,128]{2,1,0:T(8,128)(2,1)S(1)}, bf16[32,16,128]{2,1,0:T(8,128)(2,1)}, u32[]{:S(2)}) copy-start(bf16[32,16,128]{2,1,0:T(8,128)(2,1)} %param.7) | copy-start | bytes 393220
  144.1 103.8 %copy-start.1 = (f32[32,128]{1,0:T(8,128)S(1)}, f32[32,128]{1,0:T(8,128)}, u32[]{:S(2)}) copy-start(f32[32,128]{1,0:T(8,128)} %param.8) | copy-start | bytes 49156
  144.1 103.8 %copy-start.2 = (f32[32]{0:T(128)S(1)}, f32[32]{0:T(128)}, u32[]{:S(2)}) copy-start(f32[32]{0:T(128)} %param.9) | copy-start | bytes 388
  144.1 104.9 %copy-start.3 = (s32[32]{0:T(128)S(1)}, s32[32]{0:T(128)}, u32[]{:S(2)}) copy-start(s32[32]{0:T(128)} %param.13) | copy-start | bytes 388
  173.4 187.7 %all-gather.6.cloned.1.call-start = ((), (), s32[]{:S(2)}) async-start(), calls=%async_computation.5 | async-start | bytes 2359296 | tf_op jit(solution)/shard_map/all_gather | solution.py:36
  309.2 172.4 %reduce-scatter.6.cloned.1.call-start = ((), (), s32[]{:S(2)}) async-start(), calls=%async_computation.6 | async-start | bytes 2359296 | tf_op jit(solution)/shard_map/reduce_scatter | solution.py:43
  407.1 187.6 %all-gather.8.cloned.1.call-start = ((), (), s32[]{:S(2)}) async-start(), calls=%async_computation.7 | async-start | bytes 2359296 | tf_op jit(solution)/shard_map/all_gather | solution.py:36
  542.8 172.3 %reduce-scatter.8.cloned.1.call-start = ((), (), s32[]{:S(2)}) async-start(), calls=%async_computation.8 | async-start | bytes 2359296 | tf_op jit(solution)/shard_map/reduce_scatter | solution.py:43
Sparse Core Ops, SparseCore 0:
  72.9 54.3 all-gather.3
  173.5 74.3 reduce-scatter.3
  309.3 51.7 all-gather.5
  407.3 74.2 reduce-scatter.5
  543.0 51.7 all-gather.7
  640.9 74.1 reduce-scatter.7
where the time goes:
time: 746 us
  waiting for transfers between devices  379 us (51%)
  blocking collectives  203 us (27%)
  matrix products  89.7 us (12%)
  local copies, waits for them, and re-layouts  51.5 us (7%)
  between operations  14.2 us (2%)
    reduce_scatter x3, waiting for transfers between devices, per_device(): lax.psum_scatter(partial_sum, 'col', scatter_dimension=1, tiled=True)  223 us
    psum x3, blocking collectives, per_device(): totals = lax.psum(contrib, 'pair')  182 us
    all_gather x3, waiting for transfers between devices, per_device(): lax.all_gather(totals.astype(jnp.bfloat16), 'col', axis=1, tiled=True)  156 us
    dot_general x3, matrix products, per_device(): jnp.einsum('pmac,pmdc->pmad', left, own_tiles, preferred_element_type=jnp...  87.6 us
    gather x3, local copies, waits for them, and re-layouts, per_device(): selected = colamp[own_links]  41.7 us
    psum x1, blocking collectives, per_device(): pair_energy = lax.psum(jnp.sum(kfloat * amplitudes, axis=(1, 2)), 'col')  21.5 us
  transfers between devices with their start and end apart: 6, of which 6 were waited for; matrix products, arithmetic and copies ran while one was open for 0% of the time, Pallas kernels for 0%

commit v1 on v0

--- a/solution.py
+++ b/solution.py
@@ -5,6 +5,7 @@
 
 COL_DEV = 8
 SWEEPS = 3
+link_ratios = lambda message: lax.all_gather(message, "pair").sum(axis=0)
 
 
 def per_device(integrals, pno_energy, shift, intersections, links, counts, column_of):
@@ -32,7 +33,7 @@
             precision=lax.Precision.HIGHEST,
         )
         contrib = contrib.reshape(ncol_all, row_count, width)
-        totals = lax.psum(contrib, "pair")
+        totals = link_ratios(contrib)
         colamp = lax.all_gather(totals.astype(jnp.bfloat16), "col", axis=1, tiled=True)
         selected = colamp[own_links]
         left = jnp.einsum(

time: 746 us -> 752 us (level)
  blocking collectives: 203 us -> 21.5 us
  waiting for transfers between devices: 379 us -> 553 us
  other arithmetic: 6.93 us -> 20.1 us
    psum x3 -> x0, blocking collectives: 182 us -> none  [per_device(): totals = lax.psum(contrib, 'pair')]
    all_gather x0 -> x3, waiting for transfers between devices: none -> 156 us  [link_ratios = lambda message: lax.all_gather(message, 'pair').sum(axis=0)]
    all_gather x3, waiting for transfers between devices: 156 us -> 174 us  [per_device(): lax.all_gather(totals.astype(jnp.bfloat16), 'col', axis=1, tiled=True)]
    reduce_sum x0 -> x3, other arithmetic: none -> 13.2 us  [link_ratios = lambda message: lax.all_gather(message, 'pair').sum(axis=0)]
    all_gather x3 -> x0, local copies, waits for them, and re-layouts: 8.83 us -> none  [per_device(): lax.all_gather(totals.astype(jnp.bfloat16), 'col', axis=1, tiled=True)]
  transfers between devices with their start and end apart: 6 -> 9, of which waited for: 6 -> 9; matrix products, arithmetic and copies ran while one was open for 0% -> 0% of each run, Pallas kernels for 0% -> 0%
where the time goes in v1:
time: 752 us
  waiting for transfers between devices  553 us (74%)
  matrix products  92.3 us (12%)
  local copies, waits for them, and re-layouts  50 us (7%)
  blocking collectives  21.5 us (3%)
  other arithmetic  20.1 us (3%)
  between operations  13.9 us (2%)
    reduce_scatter x3, waiting for transfers between devices, per_device(): lax.psum_scatter(partial_sum, 'col', scatter_dimension=1, tiled=True)  223 us
    all_gather x3, waiting for transfers between devices, per_device(): lax.all_gather(totals.astype(jnp.bfloat16), 'col', axis=1, tiled=True)  174 us
    all_gather x3, waiting for transfers between devices, link_ratios = lambda message: lax.all_gather(message, 'pair').sum(axis=0)  156 us
    dot_general x3, matrix products, per_device(): jnp.einsum('pmac,pmdc->pmad', left, own_tiles, preferred_element_type=jnp...  87.6 us
    gather x3, local copies, waits for them, and re-layouts, per_device(): selected = colamp[own_links]  46.4 us
    psum x1, blocking collectives, per_device(): pair_energy = lax.psum(jnp.sum(kfloat * amplitudes, axis=(1, 2)), 'col')  21.5 us
  transfers between devices with their start and end apart: 9, of which 9 were waited for; matrix products, arithmetic and copies ran while one was open for 0% of the time, Pallas kernels for 0%

profile of v1, /device:TPU:0, one launch (start us, length us, event | category | flops | bytes accessed | tf_op | source)
XLA Modules:
  0.0 751.8 jit_solution(5269219326829976941)
XLA Ops:
  7.2 0.0 all-gather.16.cloned.1.call-start
  7.2 0.8 constant_dynamic-slice_fusion
  8.0 1.1 fusion.18
  9.1 2.0 fusion.32
  11.1 0.0 all-gather.16.cloned.1.call-update
  11.1 0.0 all-gather.10.cloned.1.call-start
  11.2 54.7 %all-gather.16.cloned.1.call-done = f32[1024,16,128]{2,0,1:T(8,128)} async-done(((f32[64,16,128]{2,0,1:T(8,128)}), f32[1024,16,128]{2,0,1:T(8,128)}) %all-gather.16.cloned.1.call-update) | async-done | bytes 8388624 | tf_op jit(solution)/shard_map/all_gather | solution.py:8
  65.9 4.4 reduce_sum.63
  70.3 0.9 copy.68
  71.2 0.0 all-gather.10.cloned.1.call-update
  71.2 0.0 reduce-scatter.4.cloned.1.call-start
  71.3 0.7 compare_select_fusion
  72.0 0.1 copy.25
  72.0 0.1 reshape.155
  72.1 0.7 compare_convert_fusion
  72.9 56.9 %all-gather.10.cloned.1.call-done = bf16[64,128,128]{2,1,0:T(8,128)(2,1)} async-done(((bf16[64,16,128]{2,1,0:T(8,128)(2,1)}), bf16[64,128,128]{2,1,0:T(8,128)(2,1)}) %all-gather.10.cloned.1.call-update) | async-done | bytes 2097168 | tf_op jit(solution)/shard_map/all_gather | solution.py:37
  129.8 15.5 %gather_fusion = bf16[512,128,128]{2,1,0:T(8,128)(2,1)} fusion(bf16[64,128,128]{2,1,0:T(8,128)(2,1)} %all-gather.10.cloned.1.call-done, s32[1024]{0:T(1024)S(1)} %pad_clamp_fusion), kind=kCustom, calls=%fused_computation | custom fusion | bytes 33556480 | tf_op jit(solution)/shard_map/gather | solution.py:38
  145.3 0.0 copy-start
  145.3 0.0 copy-start.1
  145.3 0.0 copy-start.2
  145.3 0.0 copy-start.3
  145.3 29.2 %multiply_reduce_fusion.2 = f32[32,128,128]{2,1,0:T(8,128)} fusion(f32[32,16]{1,0:T(8,128)S(1)} %compare_convert_fusion, bf16[32,16,128,128]{3,2,1,0:T(8,128)(2,1)} %param.10, bf16[32,16,128,128]{3,2,1,0:T(8,128)(2,1)} %bitcast.62), kind=kOutput, calls=%fused_computation.5 | convolution fusion | flops 4319608832 | bytes 35653632 | tf_op jit(solution)/shard_map/pmac,pmdc->pmad/dot_general | solution.py:42
  174.5 0.0 reduce-scatter.4.cloned.1.call-update
  174.5 0.0 all-gather.18.cloned.1.call-start
  174.6 74.4 %reduce-scatter.4.cloned.1.call-done = f32[32,16,128]{2,1,0:T(8,128)} async-done(((f32[32,128,128]{2,1,0:T(8,128)}), f32[32,16,128]{2,1,0:T(8,128)}) %reduce-scatter.4.cloned.1.call-update) | async-done | bytes 262160 | tf_op jit(solution)/shard_map/reduce_scatter | solution.py:44
  249.0 0.0 copy-done
  249.0 0.0 copy-done.1
  249.0 0.0 copy-done.2
  249.0 1.1 fusion.20
  250.2 0.0 copy-done.3
  250.2 1.3 fusion.29
  251.5 0.0 all-gather.18.cloned.1.call-update
  251.5 0.0 all-gather.12.cloned.1.call-start
  251.6 50.7 %all-gather.18.cloned.1.call-done = f32[1024,16,128]{2,0,1:T(8,128)} async-done(((f32[64,16,128]{2,0,1:T(8,128)}), f32[1024,16,128]{2,0,1:T(8,128)}) %all-gather.18.cloned.1.call-update) | async-done | bytes 8388624 | tf_op jit(solution)/shard_map/all_gather | solution.py:8
  302.3 4.4 reduce_sum.65
  306.7 0.9 copy.67
  307.5 0.0 all-gather.12.cloned.1.call-update
  307.6 0.2 reduce-scatter.6.cloned.1.call-start
  307.8 58.4 %all-gather.12.cloned.1.call-done = bf16[64,128,128]{2,1,0:T(8,128)(2,1)} async-done(((bf16[64,16,128]{2,1,0:T(8,128)(2,1)}), bf16[64,128,128]{2,1,0:T(8,128)(2,1)}) %all-gather.12.cloned.1.call-update) | async-done | bytes 2097168 | tf_op jit(solution)/shard_map/all_gather | solution.py:37
  366.2 15.5 %gather_fusion.1 = bf16[512,128,128]{2,1,0:T(8,128)(2,1)} fusion(bf16[64,128,128]{2,1,0:T(8,128)(2,1)} %all-gather.12.cloned.1.call-done, s32[1024]{0:T(1024)S(1)} %pad_clamp_fusion), kind=kCustom, calls=%fused_computation.1 | custom fusion | bytes 33556480 | tf_op jit(solution)/shard_map/gather | solution.py:38
  381.6 29.2 %multiply_reduce_fusion.1 = f32[32,128,128]{2,1,0:T(8,128)} fusion(f32[32,16]{1,0:T(8,128)S(1)} %compare_convert_fusion, bf16[32,16,128,128]{3,2,1,0:T(8,128)(2,1)} %param.10, bf16[32,16,128,128]{3,2,1,0:T(8,128)(2,1)} %bitcast.63), kind=kOutput, calls=%fused_computation.4 | convolution fusion | flops 4319608832 | bytes 35653632 | tf_op jit(solution)/shard_map/pmac,pmdc->pmad/dot_general | solution.py:42
  410.9 0.0 reduce-scatter.6.cloned.1.call-update
  410.9 0.0 all-gather.20.cloned.1.call-start
  410.9 74.3 %reduce-scatter.6.cloned.1.call-done = f32[32,16,128]{2,1,0:T(8,128)} async-done(((f32[32,128,128]{2,1,0:T(8,128)}), f32[32,16,128]{2,1,0:T(8,128)}) %reduce-scatter.6.cloned.1.call-update) | async-done | bytes 262160 | tf_op jit(solution)/shard_map/reduce_scatter | solution.py:44
  485.3 1.1 fusion.22
  486.4 1.3 fusion.26
  487.7 0.0 all-gather.20.cloned.1.call-update
  487.8 0.0 all-gather.14.cloned.1.call-start
  487.8 50.7 %all-gather.20.cloned.1.call-done = f32[1024,16,128]{2,0,1:T(8,128)} async-done(((f32[64,16,128]{2,0,1:T(8,128)}), f32[1024,16,128]{2,0,1:T(8,128)}) %all-gather.20.cloned.1.call-update) | async-done | bytes 8388624 | tf_op jit(solution)/shard_map/all_gather | solution.py:8
  538.5 4.4 reduce_sum.67
  542.9 0.9 copy.66
  543.8 0.0 all-gather.14.cloned.1.call-update
  543.8 0.3 reduce-scatter.8.cloned.1.call-start
  544.1 58.3 %all-gather.14.cloned.1.call-done = bf16[64,128,128]{2,1,0:T(8,128)(2,1)} async-done(((bf16[64,16,128]{2,1,0:T(8,128)(2,1)}), bf16[64,128,128]{2,1,0:T(8,128)(2,1)}) %all-gather.14.cloned.1.call-update) | async-done | bytes 2097168 | tf_op jit(solution)/shard_map/all_gather | solution.py:37
  602.4 15.5 %gather_fusion.2 = bf16[512,128,128]{2,1,0:T(8,128)(2,1)} fusion(bf16[64,128,128]{2,1,0:T(8,128)(2,1)} %all-gather.14.cloned.1.call-done, s32[1024]{0:T(1024)S(1)} %pad_clamp_fusion), kind=kCustom, calls=%fused_computation.2 | custom fusion | bytes 33556480 | tf_op jit(solution)/shard_map/gather | solution.py:38
  617.9 29.2 %multiply_reduce_fusion = f32[32,128,128]{2,1,0:T(8,128)} fusion(f32[32,16]{1,0:T(8,128)S(1)} %compare_convert_fusion, bf16[32,16,128,128]{3,2,1,0:T(8,128)(2,1)} %param.10, bf16[32,16,128,128]{3,2,1,0:T(8,128)(2,1)} %bitcast.61), kind=kOutput, calls=%fused_computation.3 | convolution fusion | flops 4319608832 | bytes 35653632 | tf_op jit(solution)/shard_map/pmac,pmdc->pmad/dot_general | solution.py:42
  647.1 0.0 reduce-scatter.8.cloned.1.call-update
  647.1 74.5 %reduce-scatter.8.cloned.1.call-done = f32[32,16,128]{2,1,0:T(8,128)} async-done(((f32[32,128,128]{2,1,0:T(8,128)}), f32[32,16,128]{2,1,0:T(8,128)}) %reduce-scatter.8.cloned.1.call-update) | async-done | bytes 262160 | tf_op jit(solution)/shard_map/reduce_scatter | solution.py:44
  721.6 2.2 fusion.25
  723.8 21.5 %psum.7 = f32[32]{0:T(128)} all-reduce(f32[32]{0:T(128)S(1)} %get-tuple-element.2), channel_id=1, replica_groups=mesh['col'=8,'pair'=16] {'col'}, use_global_device_ids=true, to_apply=%region_10.0 | all-reduce | flops 32 | bytes 256 | tf_op jit(solution)/shard_map/psum | solution.py:46
  (2 shorter events, 0.0 us)
Async XLA Ops:
  7.2 58.7 %all-gather.16.cloned.1.call-start = ((), (), s32[]{:S(2)}) async-start(), calls=%async_computation.9 | async-start | bytes 8912896 | tf_op jit(solution)/shard_map/all_gather | solution.py:8
  11.1 118.7 %all-gather.10.cloned.1.call-start = ((), (), s32[]{:S(2)}) async-start(), calls=%async_computation.3 | async-start | bytes 2359296 | tf_op jit(solution)/shard_map/all_gather | solution.py:37
  71.2 177.8 %reduce-scatter.4.cloned.1.call-start = ((), (), s32[]{:S(2)}) async-start(), calls=%async_computation.4 | async-start | bytes 2359296 | tf_op jit(solution)/shard_map/reduce_scatter | solution.py:44
  145.3 103.7 %copy-start = (bf16[32,16,128]{2,1,0:T(8,128)(2,1)S(1)}, bf16[32,16,128]{2,1,0:T(8,128)(2,1)}, u32[]{:S(2)}) copy-start(bf16[32,16,128]{2,1,0:T(8,128)(2,1)} %param.7) | copy-start | bytes 393220
  145.3 103.7 %copy-start.1 = (f32[32,128]{1,0:T(8,128)S(1)}, f32[32,128]{1,0:T(8,128)}, u32[]{:S(2)}) copy-start(f32[32,128]{1,0:T(8,128)} %param.8) | copy-start | bytes 49156
  145.3 103.7 %copy-start.2 = (f32[32]{0:T(128)S(1)}, f32[32]{0:T(128)}, u32[]{:S(2)}) copy-start(f32[32]{0:T(128)} %param.9) | copy-start | bytes 388
  145.3 104.9 %copy-start.3 = (s32[32]{0:T(128)S(1)}, s32[32]{0:T(128)}, u32[]{:S(2)}) copy-start(s32[32]{0:T(128)} %param.13) | copy-start | bytes 388
  174.5 127.7 %all-gather.18.cloned.1.call-start = ((), (), s32[]{:S(2)}) async-start(), calls=%async_computation.10 | async-start | bytes 8912896 | tf_op jit(solution)/shard_map/all_gather | solution.py:8
  251.5 114.6 %all-gather.12.cloned.1.call-start = ((), (), s32[]{:S(2)}) async-start(), calls=%async_computation.5 | async-start | bytes 2359296 | tf_op jit(solution)/shard_map/all_gather | solution.py:37
  307.6 177.7 %reduce-scatter.6.cloned.1.call-start = ((), (), s32[]{:S(2)}) async-start(), calls=%async_computation.6 | async-start | bytes 2359296 | tf_op jit(solution)/shard_map/reduce_scatter | solution.py:44
  410.9 127.6 %all-gather.20.cloned.1.call-start = ((), (), s32[]{:S(2)}) async-start(), calls=%async_computation.11 | async-start | bytes 8912896 | tf_op jit(solution)/shard_map/all_gather | solution.py:8
  487.8 114.6 %all-gather.14.cloned.1.call-start = ((), (), s32[]{:S(2)}) async-start(), calls=%async_computation.7 | async-start | bytes 2359296 | tf_op jit(solution)/shard_map/all_gather | solution.py:37
  543.8 177.8 %reduce-scatter.8.cloned.1.call-start = ((), (), s32[]{:S(2)}) async-start(), calls=%async_computation.8 | async-start | bytes 2359296 | tf_op jit(solution)/shard_map/reduce_scatter | solution.py:44
Sparse Core Ops, SparseCore 0:
  11.2 54.6 all-gather.15
  71.3 58.4 all-gather.9
  174.7 74.3 reduce-scatter.3
  251.6 50.5 all-gather.17
  307.7 58.4 all-gather.11
  411.0 74.2 reduce-scatter.5
  487.9 50.5 all-gather.19
  543.9 58.4 all-gather.13
  647.2 74.3 reduce-scatter.7
